TPU v7x, 512 devices: a whole 4x8x8 slice. The times are simulated.
512 devices in a mesh: wide: 32 (over z, x), narrow: 16 (over y, core).
Axes of the slice: x: 4, y: 8, z: 8, core: 2. Of those that a mesh axis runs over, the one named last changes fastest.
Arguments:
- tokens: bfloat16 [1024, 16384], P('wide', 'narrow'), may hold values from -200 to 200
- norm_gain: float32 [16384], P('narrow'), may hold values from 0.25 to 1.75
- gate_weight: bfloat16 [26624, 16384], P('wide', 'narrow'), may hold values from -0.046875 to 0.046875
- up_weight: bfloat16 [26624, 16384], P('wide', 'narrow'), may hold values from -0.046875 to 0.046875
- down_weight: bfloat16 [26624, 16384], P('wide', 'narrow'), may hold values from -0.0390625 to 0.0390625
Outputs:
- ffn_out: bfloat16 [1024, 16384], P('wide', 'narrow')
All inputs are finite; a program needn't handle non-finite values.
Results may differ from a plain program's by a relative error of at most 0.03.
Values may be sent and summed in bfloat16 or wider, within the bound.
No kernel may reach another device: no remote copies, remote signals or barrier semaphores. Data moves between devices by JAX's collectives and lax.ppermute only.
A program may use at most 64 MiB of HBM per device.

v0:
```python
import jax
import jax.numpy as jnp
from jax import lax
from jax.sharding import PartitionSpec as P

D = 16384
EPS = 1e-05


def project_pair(rows, gate_weight, up_weight):
    dims = (((1,), (1,)), ((), ()))
    gate = lax.dot_general(rows, gate_weight, dims, preferred_element_type=jnp.float32)
    upward = lax.dot_general(rows, up_weight, dims, preferred_element_type=jnp.float32)
    return jnp.concatenate([gate, upward], axis=1)


def activate(sums, width):
    return (jax.nn.silu(sums[:, :width]) * sums[:, width:]).astype(jnp.bfloat16)


def local(tokens, norm_gain, gate_weight, up_weight, down_weight):
    width = gate_weight.shape[0]
    whole = lax.all_gather(tokens, "wide", axis=0, tiled=True)
    values = whole.astype(jnp.float32)
    squares = lax.psum(jnp.sum(values * values, axis=1), "narrow")
    normed = (values * lax.rsqrt(squares[:, None] / D + EPS) * norm_gain).astype(jnp.bfloat16)
    sums = lax.psum(
        project_pair(normed, gate_weight, up_weight).astype(jnp.bfloat16), "narrow"
    ).astype(jnp.float32)
    hidden = activate(sums, width)
    return lax.psum_scatter(
        jnp.dot(hidden, down_weight, preferred_element_type=jnp.float32).astype(jnp.bfloat16),
        "wide",
        scatter_dimension=0,
        tiled=True,
    )


def solution(mesh):
    in_specs = (
        P("wide", "narrow"),
        P("narrow"),
        P("wide", "narrow"),
        P("wide", "narrow"),
        P("wide", "narrow"),
    )
    out_specs = P("wide", "narrow")
    return jax.shard_map(local, mesh=mesh, in_specs=in_specs, out_specs=out_specs, check_vma=False)
```

profile of v0, /device:TPU:8, one launch (start us, length us, event | category | flops | bytes accessed | tf_op | source)
XLA Modules:
  0.0 490.7 jit_solution(1981325503855157326)
XLA Ops:
  6.5 0.0 copy-start
  6.5 0.0 all-gather.2.cloned.1.call-start
  6.5 0.7 all-gather.2.cloned.1.call-update
  7.3 0.0 all-reduce.2.cloned.1.call-start
  7.3 91.8 %all-gather.2.cloned.1.call-done = bf16[1024,1024]{1,0:T(8,128)(2,1)} async-done(((bf16[32,1024]{1,0:T(8,128)(2,1)}), bf16[1024,1024]{1,0:T(8,128)(2,1)}) %all-gather.2.cloned.1.call-update) | async-done | bytes 2097168 | tf_op jit(solution)/shard_map/all_gather | solution.py:23
  99.1 2.1 fusion
  101.2 20.6 %psum.14 = f32[1024]{0:T(1024)S(1)} all-reduce(f32[1024]{0:T(1024)S(1)} %fusion), channel_id=1, replica_groups=mesh['wide'=32,'narrow'=16] {'narrow'}, use_global_device_ids=true, to_apply=%region_1.0 | all-reduce | flops 1024 | bytes 8192 | tf_op jit(solution)/shard_map/psum | solution.py:25
  121.8 0.0 copy-start.1
  121.8 0.0 copy-start.2
  121.8 0.0 copy-start.3
  121.9 4.3 convolution_convert_fusion.1
  126.2 0.0 copy-done.1
  126.2 0.0 copy-done.2
  126.2 0.0 copy-done.3
  126.2 2.1 convolution_convert_fusion.2
  128.3 2.1 pad_maximum_fusion
  130.4 0.0 all-reduce.2.cloned.1.call-update
  130.4 0.0 reduce-scatter.2.cloned.1.call-start
  130.5 121.9 %all-reduce.2.cloned.1.call-done = bf16[1024,1664]{0,1:T(8,128)(2,1)} async-done(((bf16[1024,1664]{0,1:T(8,128)(2,1)}), bf16[1024,1664]{0,1:T(8,128)(2,1)}) %all-reduce.2.cloned.1.call-update) | async-done | bytes 3407888 | tf_op jit(solution)/shard_map/psum | solution.py:27
  252.4 2.8 convert_element_type.18
  255.2 0.0 copy-done
  255.2 3.9 convolution_convert_fusion
  259.0 0.0 reduce-scatter.2.cloned.1.call-update
  259.1 225.1 %reduce-scatter.2.cloned.1.call-done = bf16[32,1024]{1,0:T(8,128)(2,1)} async-done(((bf16[1024,1024]{1,0:T(8,128)(2,1)}), bf16[32,1024]{1,0:T(8,128)(2,1)}) %reduce-scatter.2.cloned.1.call-update) | async-done | bytes 65552 | tf_op jit(solution)/shard_map/reduce_scatter | solution.py:31
  (1 shorter events, 0.0 us)
Async XLA Ops:
  6.5 248.6 %copy-start = (bf16[832,1024]{1,0:T(8,128)(2,1)S(1)}, bf16[832,1024]{1,0:T(8,128)(2,1)}, u32[]{:S(2)}) copy-start(bf16[832,1024]{1,0:T(8,128)(2,1)} %param.9) | copy-start | bytes 5111812
  6.5 92.6 %all-gather.2.cloned.1.call-start = ((), (), s32[]{:S(2)}) async-start(), calls=%async_computation.1 | async-start | bytes 2162688 | tf_op jit(solution)/shard_map/all_gather | solution.py:23
  7.3 245.1 %all-reduce.2.cloned.1.call-start = ((), (), s32[]{:S(2)}) async-start(), calls=%async_computation.2 | async-start | bytes 6815744 | tf_op jit(solution)/shard_map/psum | solution.py:27
  121.8 4.3 copy-start.1
  121.8 4.3 copy-start.2
  121.8 4.3 copy-start.3
  130.4 353.8 %reduce-scatter.2.cloned.1.call-start = ((), (), s32[]{:S(2)}) async-start(), calls=%async_computation.3 | async-start | bytes 2162688 | tf_op jit(solution)/shard_map/reduce_scatter | solution.py:31
Sparse Core Ops, SparseCore 0:
  10.5 88.5 all-gather.1
  130.6 121.7 all-reduce.1
  259.2 224.9 reduce-scatter.1
where the time goes:
time: 491 us
  waiting for transfers between devices  440 us (90%)
  blocking collectives  20.6 us (4%)
  between operations  13.2 us (3%)
  matrix products  10.3 us (2%)
  other arithmetic  6.94 us (1%)
    reduce_scatter x1, waiting for transfers between devices, local(): lax.psum_scatter(jnp.dot(hidden, down_weight, preferred_element_type=jnp....  225 us
    psum x1, waiting for transfers between devices, local(): lax.psum(project_pair(normed, gate_weight, up_weight).astype(jnp.bfloat16...  122 us
    all_gather x1, waiting for transfers between devices, local(): whole = lax.all_gather(tokens, 'wide', axis=0, tiled=True)  91.8 us
    psum x1, blocking collectives, local(): squares = lax.psum(jnp.sum(values * values, axis=1), 'narrow')  20.6 us
  transfers between devices with their start and end apart: 3, of which 3 were waited for; matrix products, arithmetic and copies ran while one was open for 0% of the time, Pallas kernels for 0%

commit v1 on v0

--- a/solution.py
+++ b/solution.py
@@ -20,7 +20,9 @@
 
 def local(tokens, norm_gain, gate_weight, up_weight, down_weight):
     width = gate_weight.shape[0]
-    whole = lax.all_gather(tokens, "wide", axis=0, tiled=True)
+    whole = jnp.concatenate(
+        lax.all_to_all(jnp.stack([tokens] * lax.axis_size("wide")), "wide", 0, 0), axis=0
+    )
     values = whole.astype(jnp.float32)
     squares = lax.psum(jnp.sum(values * values, axis=1), "narrow")
     normed = (values * lax.rsqrt(squares[:, None] / D + EPS) * norm_gain).astype(jnp.bfloat16)

time: 491 us -> 463 us (0.943)
  waiting for transfers between devices: 440 us -> 346 us
  blocking collectives: 20.6 us -> 84.8 us
    all_gather x1 -> x0, waiting for transfers between devices: 91.8 us -> none  [local(): whole = lax.all_gather(tokens, 'wide', axis=0, tiled=True)]
    all_to_all x0 -> x1, blocking collectives: none -> 63.5 us  [local(): lax.all_to_all(jnp.stack([tokens] * lax.axis_size('wide')), 'wide', 0, 0)]
  transfers between devices with their start and end apart: 3 -> 2, of which waited for: 3 -> 2; matrix products, arithmetic and copies ran while one was open for 0% -> 0% of each run, Pallas kernels for 0% -> 0%
where the time goes in v1:
time: 463 us
  waiting for transfers between devices  346 us (75%)
  blocking collectives  84.8 us (18%)
  between operations  13.5 us (3%)
  matrix products  7.9 us (2%)
  other arithmetic  7.6 us (2%)
    reduce_scatter x1, waiting for transfers between devices, local(): lax.psum_scatter(jnp.dot(hidden, down_weight, preferred_element_type=jnp....  225 us
    psum x1, waiting for transfers between devices, local(): lax.psum(project_pair(normed, gate_weight, up_weight).astype(jnp.bfloat16...  121 us
    all_to_all x1, blocking collectives, local(): lax.all_to_all(jnp.stack([tokens] * lax.axis_size('wide')), 'wide', 0, 0)  63.5 us
    psum x1, blocking collectives, local(): squares = lax.psum(jnp.sum(values * values, axis=1), 'narrow')  21.2 us
  transfers between devices with their start and end apart: 2, of which 2 were waited for; matrix products, arithmetic and copies ran while one was open for 0% of the time, Pallas kernels for 0%

profile of v1, /device:TPU:8, one launch (start us, length us, event | category | flops | bytes accessed | tf_op | source)
XLA Modules:
  0.0 462.8 jit_solution(7485414060389519266)
XLA Ops:
  6.5 0.0 copy-start
  6.5 0.0 all-reduce.2.cloned.1.call-start
  6.5 1.2 stack.2
  7.8 63.5 %all_to_all.5 = bf16[32,32,1024]{2,1,0:T(8,128)(2,1)S(1)} all-to-all(bf16[32,32,1024]{2,1,0:T(8,128)(2,1)S(1)} %stack.2), channel_id=1, replica_groups=mesh['wide'=32,'narrow'=16] {'wide'}, dimensions={0} | all-to-all | bytes 4194304 | tf_op jit(solution)/shard_map/all_to_all | solution.py:24
  71.3 1.3 copy-done.1
  72.6 0.5 multiply_reduce_fusion
  73.1 0.1 reduce_sum.12
  73.2 21.2 %psum.14 = f32[1024]{0:T(1024)S(1)} all-reduce(f32[1024]{0:T(1024)S(1)} %reduce_sum.12), channel_id=1, replica_groups=mesh['wide'=32,'narrow'=16] {'narrow'}, use_global_device_ids=true, to_apply=%region_1.0 | all-reduce | flops 1024 | bytes 8192 | tf_op jit(solution)/shard_map/psum | solution.py:27
  94.4 0.0 copy-done.2
  94.4 0.0 copy-start.3
  94.5 2.3 fusion.1
  96.7 0.0 copy-done.3
  96.7 0.0 copy-start.4
  96.7 2.0 convolution_convert_fusion.1
  98.8 2.0 convolution_convert_fusion.2
  100.8 2.1 pad_maximum_fusion
  102.9 0.0 all-reduce.2.cloned.1.call-update
  102.9 0.0 reduce-scatter.2.cloned.1.call-start
  103.0 121.4 %all-reduce.2.cloned.1.call-done = bf16[1024,1664]{0,1:T(8,128)(2,1)} async-done(((bf16[1024,1664]{0,1:T(8,128)(2,1)}), bf16[1024,1664]{0,1:T(8,128)(2,1)}) %all-reduce.2.cloned.1.call-update) | async-done | bytes 3407888 | tf_op jit(solution)/shard_map/psum | solution.py:29
  224.3 2.8 convert_element_type.26
  227.1 0.0 copy-done
  227.1 3.9 convolution_convert_fusion
  231.0 0.0 reduce-scatter.2.cloned.1.call-update
  231.0 224.9 %reduce-scatter.2.cloned.1.call-done = bf16[32,1024]{1,0:T(8,128)(2,1)} async-done(((bf16[1024,1024]{1,0:T(8,128)(2,1)}), bf16[32,1024]{1,0:T(8,128)(2,1)}) %reduce-scatter.2.cloned.1.call-update) | async-done | bytes 65552 | tf_op jit(solution)/shard_map/reduce_scatter | solution.py:33
  (4 shorter events, 0.0 us)
Async XLA Ops:
  6.5 220.6 %copy-start = (bf16[832,1024]{1,0:T(8,128)(2,1)S(1)}, bf16[832,1024]{1,0:T(8,128)(2,1)}, u32[]{:S(2)}) copy-start(bf16[832,1024]{1,0:T(8,128)(2,1)} %param.9) | copy-start | bytes 5111812
  6.5 217.8 %all-reduce.2.cloned.1.call-start = ((), (), s32[]{:S(2)}) async-start(), calls=%async_computation.2 | async-start | bytes 6815744 | tf_op jit(solution)/shard_map/psum | solution.py:29
  71.3 1.4 copy-start.1
  72.6 21.8 %copy-start.2 = (f32[1024]{0:T(1024)S(1)}, f32[1024]{0:T(1024)}, u32[]{:S(2)}) copy-start(f32[1024]{0:T(1024)} %param.6) | copy-start | bytes 12292
  94.4 2.3 copy-start.3
  96.7 2.0 copy-start.4
  102.9 353.0 %reduce-scatter.2.cloned.1.call-start = ((), (), s32[]{:S(2)}) async-start(), calls=%async_computation.3 | async-start | bytes 2162688 | tf_op jit(solution)/shard_map/reduce_scatter | solution.py:33
Sparse Core Ops, SparseCore 0:
  103.0 121.2 all-reduce.1
  231.1 224.7 reduce-scatter.1
